TPU v7x, 128 devices: a whole 4x4x4 slice. The times are simulated.
128 devices in a mesh: blk: 16 (over x, y_hi, core), req: 8 (over y_lo, z).
Axes of the slice: x: 4, y: 4 (y_hi: 2, y_lo: 2; y = y_hi * 2 + y_lo), z: 4, core: 2. Of those that a mesh axis runs over, the one named last changes fastest.
Arguments:
- long_q: bfloat16 [16384, 2048], P('blk', 'req'), may hold values from -6 to 6
- long_k: bfloat16 [16384, 2048], P('blk', 'req'), may hold values from -6 to 6
- long_v: bfloat16 [16384, 2048], P('blk', 'req'), may hold values from -6 to 6
- short_q: bfloat16 [8192, 2048], P('blk', 'req'), may hold values from -6 to 6
- short_k: bfloat16 [8192, 2048], P('blk', 'req'), may hold values from -6 to 6
- short_v: bfloat16 [8192, 2048], P('blk', 'req'), may hold values from -6 to 6
- short_seg: int32 [16, 512], P('blk'), may hold values from 0 to 15, never falling along the last dimension, each value on 1 to 96 neighbouring positions
- pool_kv: bfloat16 [1024, 2, 16, 2048], P('blk', None, None, 'req'), may hold values from -6 to 6
- page_table: int32 [16, 16, 4], replicated, may hold values from 0 to 1023, as said below
- w_out: bfloat16 [2048, 2048], replicated, may hold values from -0.125 to 0.125
Outputs:
- long_out: bfloat16 [16384, 2048], P(('blk', 'req'))
- short_out: bfloat16 [8192, 2048], P(('blk', 'req'))
Inputs may be any that keep to these rules, and one draw needn't show every extreme that they name: `short_seg`: along each pack the request numbers never fall, and each of the 16 requests has 1 to 96 tokens, one of them exactly 96. `page_table`: entry [b, s, j] is o * 64 + i for page i of the pool rows held by index o of blk; for every pack b and every o exactly 4 of the 64 entries of b name pages of o.
All inputs are finite; a program needn't handle non-finite values.
Results may differ from a plain program's by a relative error of at most 0.015.
Values may be sent and summed in bfloat16 or wider, within the bound.
No kernel may reach another device: no remote copies, remote signals or barrier semaphores. Data moves between devices by JAX's collectives and lax.ppermute only.
A program may use at most 128 MiB of HBM per device.

v0:
```python
import math
import jax
import jax.numpy as jnp
from jax import lax
from jax.sharding import PartitionSpec as P

HD = 128
PPS = 4
very_negative = -1e30


def fold_block(state_now, query_heads, query_pos, key_block, value_block, block_first):
    acc_sum, run_max, run_total = state_now
    heads_dev = query_heads.shape[1]
    key_heads = key_block.reshape(key_block.shape[0], heads_dev, HD)
    value_heads = value_block.reshape(value_block.shape[0], heads_dev, HD)
    scores = jnp.einsum(
        "qhd,khd->hqk", query_heads, key_heads, preferred_element_type=jnp.float32
    ) * HD ** (-0.5)
    key_pos = block_first + jnp.arange(key_block.shape[0], dtype=jnp.int32)
    allowed = (key_pos[None, :] <= query_pos[:, None])[None]
    scores = jnp.where(allowed, scores, very_negative)
    new_max = jnp.maximum(run_max, jnp.max(scores, axis=-1))
    weights = jnp.where(allowed, jnp.exp(scores - new_max[..., None]), 0.0)
    factor = jnp.exp(run_max - new_max)
    run_total = run_total * factor + jnp.sum(weights, axis=-1)
    acc_sum = acc_sum * factor[..., None] + jnp.einsum(
        "hqk,khd->hqd",
        weights.astype(jnp.bfloat16),
        value_heads,
        preferred_element_type=jnp.float32,
    )
    return (acc_sum, new_max, run_total)


def prompt_attention(queries, query_pos, long_k, long_v):
    row_count, width = queries.shape
    heads_dev = width // HD
    query_heads = queries.reshape(row_count, heads_dev, HD)
    last_pos = jnp.max(query_pos)
    init = (
        jnp.zeros((heads_dev, row_count, HD), jnp.float32),
        jnp.full((heads_dev, row_count), very_negative, jnp.float32),
        jnp.zeros((heads_dev, row_count), jnp.float32),
    )
    key_piece = lax.all_gather(long_k, "blk", axis=0, tiled=True)
    value_piece = lax.all_gather(long_v, "blk", axis=0, tiled=True)
    piece_rows = key_piece.shape[0]
    step_rows = math.gcd(piece_rows, 1024)

    def one_step(block_num, state_in):
        block_start = block_num * step_rows
        key_block = lax.dynamic_slice_in_dim(key_piece, block_start, step_rows, 0)
        value_block = lax.dynamic_slice_in_dim(value_piece, block_start, step_rows, 0)

        def compute_block(state_live):
            return fold_block(
                state_live, query_heads, query_pos, key_block, value_block, block_start
            )

        def keep_state(state_skip):
            return state_skip

        return lax.cond(block_start <= last_pos, compute_block, keep_state, state_in)

    acc_sum, run_max, run_total = lax.fori_loop(0, piece_rows // step_rows, one_step, init)
    merged = acc_sum / run_total[..., None]
    return merged.transpose(1, 0, 2).reshape(row_count, width).astype(jnp.bfloat16)


def pack_attention(
    short_q, short_k, short_v, short_seg, pool_kv, page_table, block_index, block_count
):
    pack_rows, width = short_q.shape
    heads_dev = width // HD
    pool_pages = pool_kv.shape[0]
    page_len = pool_kv.shape[2]
    page_rows = page_table.reshape(block_count, -1)
    entries = page_rows.shape[1]
    capacity = entries // block_count
    owners = page_rows // pool_pages
    places = page_rows % pool_pages
    wanted = owners == block_index
    ranks = jnp.cumsum(wanted.astype(jnp.int32), axis=1) - 1
    picked = wanted[:, :, None] & (
        ranks[:, :, None] == jnp.arange(capacity, dtype=jnp.int32)[None, None, :]
    )
    send_places = jnp.sum(jnp.where(picked, places[:, :, None], 0), axis=1)
    outgoing = pool_kv[send_places.reshape(-1)].reshape(block_count, capacity, 2, page_len, width)
    arrived = lax.all_to_all(outgoing, "blk", split_axis=0, concat_axis=0, tiled=True)
    my_owners = lax.dynamic_index_in_dim(owners, block_index, 0, keepdims=False)
    order = jnp.arange(entries, dtype=jnp.int32)
    before = (my_owners[None, :] == my_owners[:, None]) & (order[None, :] < order[:, None])
    slots = my_owners * capacity + jnp.sum(before.astype(jnp.int32), axis=1)
    fetched = arrived.reshape(block_count * capacity, 2, page_len, width)[slots]
    cache_len = entries * page_len
    key_rows = jnp.concatenate([fetched[:, 0].reshape(cache_len, width), short_k], 0)
    value_rows = jnp.concatenate([fetched[:, 1].reshape(cache_len, width), short_v], 0)
    segment = short_seg[0]
    positions = jnp.arange(pack_rows, dtype=jnp.int32)
    key_seg = jnp.concatenate([jnp.arange(cache_len, dtype=jnp.int32) // (PPS * page_len), segment])
    key_pos = jnp.concatenate([jnp.full((cache_len,), -1, jnp.int32), positions])
    allowed = ((key_seg[None, :] == segment[:, None]) & (key_pos[None, :] <= positions[:, None]))[
        None
    ]
    query_heads = short_q.reshape(pack_rows, heads_dev, HD)
    key_heads = key_rows.reshape(cache_len + pack_rows, heads_dev, HD)
    value_heads = value_rows.reshape(cache_len + pack_rows, heads_dev, HD)
    scores = jnp.einsum(
        "qhd,khd->hqk", query_heads, key_heads, preferred_element_type=jnp.float32
    ) * HD ** (-0.5)
    scores = jnp.where(allowed, scores, very_negative)
    row_max = jnp.max(scores, axis=-1)
    weights = jnp.where(allowed, jnp.exp(scores - row_max[..., None]), 0.0)
    total = jnp.sum(weights, axis=-1)
    numer = jnp.einsum(
        "hqk,khd->hqd",
        weights.astype(jnp.bfloat16),
        value_heads,
        preferred_element_type=jnp.float32,
    )
    merged = numer / total[..., None]
    return merged.transpose(1, 0, 2).reshape(pack_rows, width).astype(jnp.bfloat16)


def per_device(
    long_q, long_k, long_v, short_q, short_k, short_v, short_seg, pool_kv, page_table, w_out
):
    block_count = lax.axis_size("blk")
    block_index = lax.axis_index("blk")
    group_index = lax.axis_index("req")
    row_count, width = long_q.shape
    query_pos = block_index * row_count + jnp.arange(row_count, dtype=jnp.int32)
    long_attn = prompt_attention(long_q, query_pos, long_k, long_v)
    short_attn = pack_attention(
        short_q, short_k, short_v, short_seg, pool_kv, page_table, block_index, block_count
    )
    w_rows = lax.dynamic_slice_in_dim(w_out, group_index * width, width, 0)
    long_out = lax.psum_scatter(
        jnp.dot(long_attn, w_rows, preferred_element_type=jnp.float32).astype(jnp.bfloat16),
        "req",
        scatter_dimension=0,
        tiled=True,
    )
    short_out = lax.psum_scatter(
        jnp.dot(short_attn, w_rows, preferred_element_type=jnp.float32).astype(jnp.bfloat16),
        "req",
        scatter_dimension=0,
        tiled=True,
    )
    return (long_out, short_out)


def solution(mesh):
    placed = (
        P("blk", "req"),
        P("blk", "req"),
        P("blk", "req"),
        P("blk", "req"),
        P("blk", "req"),
        P("blk", "req"),
        P("blk", None),
        P("blk", None, None, "req"),
        P(),
        P(),
    )
    return jax.shard_map(
        per_device,
        mesh=mesh,
        in_specs=placed,
        out_specs=(P(("blk", "req"), None), P(("blk", "req"), None)),
        check_vma=False,
    )
```

profile of v0, /device:TPU:1, one launch (start us, length us, event | category | flops | bytes accessed | tf_op | source)
XLA Modules:
  0.0 403.9 jit_solution(17348322285215755611)
XLA Ops:
  8.1 2.1 copy.40
  10.3 2.1 copy.42
  12.4 0.8 copy.45
  13.3 0.2 reduce_window_sum.11
  13.6 0.1 select_reduce_fusion
  13.7 0.1 copy.50
  13.8 0.1 reshape.279
  13.9 1.6 gather_fusion
  15.5 8.4 %all-to-all-start = ((bf16[16,4,2,16,256]{4,3,2,1,0:T(8,128)(2,1)}), bf16[16,4,2,16,256]{4,3,2,1,0:T(8,128)(2,1)S(1)}, u32[]{:S(2)}, u32[]{:S(2)}) async-start(bf16[16,4,2,16,256]{4,3,2,1,0:T(8,128)(2,1)} %bitcast.9), calls=%async_computation.1 | async-start | bytes 2097152 | tf_op jit(solution)/shard_map/all_to_all | solution.py:90
  24.0 0.1 copy.51
  24.2 0.8 copy.53
  25.0 0.1 copy.55
  25.2 0.2 convert_reduce_fusion
  25.4 1.9 fusion.20
  27.3 17.5 %all-to-all-done = bf16[16,4,2,16,256]{4,3,2,1,0:T(8,128)(2,1)S(1)} async-done(((bf16[16,4,2,16,256]{4,3,2,1,0:T(8,128)(2,1)}), bf16[16,4,2,16,256]{4,3,2,1,0:T(8,128)(2,1)S(1)}, u32[]{:S(2)}, u32[]{:S(2)}) %all-to-all-start) | async-done | bytes 1048608 | tf_op jit(solution)/shard_map/all_to_all | solution.py:90
  44.8 0.6 gather_fusion.1
  45.4 0.9 fusion.64
  46.3 1.2 concatenate.21
  47.5 0.1 copy.52
  47.5 0.1 concatenate.24
  47.7 0.4 copy.56
  48.1 6.6 %fusion.65 = (f32[2,512]{1,0:T(2,128)S(1)}, bf16[2,512,1536]{1,2,0:T(8,128)(2,1)}) fusion(pred[512,1536]{0,1:T(8,128)(4,1)} %fusion.20, bf16[512,2,128]{2,0,1:T(8,128)(2,1)} %copy.53, bf16[1024,2,128]{2,0,1:T(8,128)(2,1)S(1)} %copy.52, bf16[512,256]{1,0:T(8,128)(2,1)} %param.17), kind=kOutput, calls=%fused_computation.93 | convolution fusion | flops 413664768 | bytes 4984832 | tf_op jit(solution)/shard_map/sub | solution.py:114
  54.7 2.5 fusion.28
  57.2 3.3 convolution_convert_fusion.1
  60.6 0.2 reduce-scatter.3.cloned.1.call-start
  60.8 0.6 add_reduce_fusion
  61.4 0.2 copy.41
  61.7 0.3 copy.43
  61.9 35.7 %all-gather.3.cloned.1.call-done = bf16[16384,256]{0,1:T(8,128)(2,1)} async-done(((bf16[1024,256]{0,1:T(8,128)(2,1)}), bf16[16384,256]{0,1:T(8,128)(2,1)}) %all-gather.3.cloned.1.call-update) | async-done | bytes 8388624 | tf_op jit(solution)/shard_map/all_gather | solution.py:46
  97.6 73.6 %all-gather.5.cloned.1.call-done = bf16[16384,256]{0,1:T(8,128)(2,1)} async-done(((bf16[1024,256]{0,1:T(8,128)(2,1)}), bf16[16384,256]{0,1:T(8,128)(2,1)}) %all-gather.5.cloned.1.call-update) | async-done | bytes 8388624 | tf_op jit(solution)/shard_map/all_gather | solution.py:47
  171.3 0.1 broadcast_in_dim.90
  171.4 30.6 %while.18 = (s32[]{:T(128)}, f32[2,1024,128]{2,1,0:T(8,128)S(1)}, f32[2,1024]{1,0:T(2,128)S(1)}, f32[2,1024]{1,0:T(2,128)S(1)}, s32[]{:T(128)}, /*index=5*/bf16[...) while((s32[]{:T(128)}, f32[2,1024,128]{2,1,0:T(8,128)S(1)}, ...), condition=%wide.region_6.7_spmd.clone, body=%wide.region_1.6_spmd.clone.sunk | while | flops 1102583808 | bytes 35283264 | solution.py:66
  172.0 10.0 %conditional.3 = ((f32[2,1024,128]{2,1,0:T(8,128)S(1)}, f32[2,1024]{1,0:T(2,128)S(1)}, f32[2,1024]{1,0:T(2,128)S(1)})) conditional(s32[]{:T(128)} %convert_element_type.77, (f32[2,1024,128]{2,1,0:T(8,128)S(1)}, f32[2,1024]{1,0:T(2,128)S(1)}, f32[2,1024]{1,0:T(2,128)S(1)}) %tuple.66, (s32[]{:T(128)}, s32[]{:T(128)}, bf16[16384,256]{0,1:T(8,128)(2,1)}, ...), branch_computations={%region_2.0_spmd, %region_3.5_spmd} | conditional | flops 1102583808 | bytes 35278928 | solution.py:64
  172.0 1.3 constant_dynamic-slice_fusion
  173.3 0.7 broadcast_compare_fusion
  174.0 2.0 fusion.2
  176.0 2.3 fusion.3
  178.3 3.7 fusion.8
  182.7 10.0 %conditional.3 = ((f32[2,1024,128]{2,1,0:T(8,128)S(1)}, f32[2,1024]{1,0:T(2,128)S(1)}, f32[2,1024]{1,0:T(2,128)S(1)})) conditional(s32[]{:T(128)} %convert_element_type.77, (f32[2,1024,128]{2,1,0:T(8,128)S(1)}, f32[2,1024]{1,0:T(2,128)S(1)}, f32[2,1024]{1,0:T(2,128)S(1)}) %tuple.66, (s32[]{:T(128)}, s32[]{:T(128)}, bf16[16384,256]{0,1:T(8,128)(2,1)}, ...), branch_computations={%region_2.0_spmd, %region_3.5_spmd} | conditional | flops 1102583808 | bytes 35278928 | solution.py:64
  182.7 1.3 constant_dynamic-slice_fusion
  184.0 0.7 broadcast_compare_fusion
  184.6 2.0 fusion.2
  186.6 2.3 fusion.3
  188.9 3.7 fusion.8
  202.0 0.3 copy.44
  202.4 0.1 divide_convert_fusion
  202.5 4.5 %convolution_convert_fusion = bf16[1024,2048]{1,0:T(8,128)(2,1)} fusion(bf16[1024,256]{0,1:T(8,128)(2,1)S(1)} %bitcast.78, bf16[2048,2048]{1,0:T(8,128)(2,1)} %param.23, s32[]{:T(128)S(6)} %select_n.90), kind=kOutput, calls=%fused_computation.25 | convolution fusion | flops 1075838976 | bytes 5767172 | tf_op jit(solution)/shard_map/dot_general | solution.py:140
  207.0 189.5 %reduce-scatter.3.cloned.1.call-done = bf16[128,2048]{1,0:T(8,128)(2,1)} async-done(((bf16[1024,2048]{1,0:T(8,128)(2,1)}), bf16[128,2048]{1,0:T(8,128)(2,1)}) %reduce-scatter.3.cloned.1.call-update) | async-done | bytes 524304 | tf_op jit(solution)/shard_map/reduce_scatter | solution.py:139
  (71 shorter events, 0.8 us)
Async XLA Ops:
  8.0 5.9 %copy-start = (bf16[64,2,16,256]{3,2,1,0:T(8,128)(2,1)S(1)}, bf16[64,2,16,256]{3,2,1,0:T(8,128)(2,1)}, u32[]{:S(2)}) copy-start(bf16[64,2,16,256]{3,2,1,0:T(8,128)(2,1)} %param.21) | copy-start | bytes 3145732
  8.0 17.4 %copy-start.4 = (s32[1536]{0:T(1024)S(1)}, s32[1536]{0:T(1024)}, u32[]{:S(2)}) copy-start(s32[1536]{0:T(1024)} %constant.138.clone.1) | copy-start | bytes 18436
  8.0 16.0 %copy-start.2 = (bf16[512,256]{1,0:T(8,128)(2,1)S(1)}, bf16[512,256]{1,0:T(8,128)(2,1)}, u32[]{:S(2)}) copy-start(bf16[512,256]{1,0:T(8,128)(2,1)} %param.18) | copy-start | bytes 786436
  8.0 17.0 %copy-start.3 = (bf16[512,256]{1,0:T(8,128)(2,1)S(1)}, bf16[512,256]{1,0:T(8,128)(2,1)}, u32[]{:S(2)}) copy-start(bf16[512,256]{1,0:T(8,128)(2,1)} %param.19) | copy-start | bytes 786436
  8.0 17.4 %copy-start.5 = (s32[1,512]{1,0:T(1,128)S(1)}, s32[1,512]{1,0:T(1,128)}, u32[]{:S(2)}) copy-start(s32[1,512]{1,0:T(1,128)} %param.20) | copy-start | bytes 6148
  8.1 89.6 %all-gather.3.cloned.1.call-start = ((), (), s32[]{:S(2)}) async-start(), calls=%async_computation.3 | async-start | bytes 8912896 | tf_op jit(solution)/shard_map/all_gather | solution.py:46
  10.3 161.0 %all-gather.5.cloned.1.call-start = ((), (), s32[]{:S(2)}) async-start(), calls=%async_computation.4 | async-start | bytes 8912896 | tf_op jit(solution)/shard_map/all_gather | solution.py:47
  15.5 29.3 %all-to-all-start = ((bf16[16,4,2,16,256]{4,3,2,1,0:T(8,128)(2,1)}), bf16[16,4,2,16,256]{4,3,2,1,0:T(8,128)(2,1)S(1)}, u32[]{:S(2)}, u32[]{:S(2)}) async-start(bf16[16,4,2,16,256]{4,3,2,1,0:T(8,128)(2,1)} %bitcast.9), calls=%async_computation.1 | async-start | bytes 2097152 | tf_op jit(solution)/shard_map/all_to_all | solution.py:90
  24.0 183.0 %reduce-scatter.5.cloned.1.call-start = ((), (), s32[]{:S(2)}) async-start(), calls=%async_computation.6 | async-start | bytes 2359296 | tf_op jit(solution)/shard_map/reduce_scatter | solution.py:145
  54.7 6.8 %copy-start.1 = (bf16[1024,256]{1,0:T(8,128)(2,1)S(1)}, bf16[1024,256]{1,0:T(8,128)(2,1)}, u32[]{:S(2)}) copy-start(bf16[1024,256]{1,0:T(8,128)(2,1)} %param.14) | copy-start | bytes 1572868
  60.6 335.9 %reduce-scatter.3.cloned.1.call-start = ((), (), s32[]{:S(2)}) async-start(), calls=%async_computation.5 | async-start | bytes 4718592 | tf_op jit(solution)/shard_map/reduce_scatter | solution.py:139
Sparse Core Ops, SparseCore 0:
  11.9 85.6 all-gather.2
  100.1 71.1 all-gather.4
Sparse Core Ops, SparseCore 1:
  60.7 49.7 reduce-scatter.4
  207.1 189.4 reduce-scatter.2
where the time goes:
time: 405 us; the launch traced here: 404 us
  waiting for transfers between devices  316 us (78%)
  matrix products  28.3 us (7%)
  between operations  15.8 us (4%)
  local copies, waits for them, and re-layouts  14.8 us (4%)
  loops' own time  10.8 us (3%)
  other arithmetic  9.14 us (2%)
  starting transfers between devices  8.79 us (2%)
    reduce_scatter x1, waiting for transfers between devices, per_device(): lax.psum_scatter(jnp.dot(long_attn, w_rows, preferred_element_type=jnp.fl...  189 us
    all_gather x1, waiting for transfers between devices, prompt_attention(): value_piece = lax.all_gather(long_v, 'blk', axis=0, tiled=True)  73.6 us
    all_gather x1, waiting for transfers between devices, prompt_attention(): key_piece = lax.all_gather(long_k, 'blk', axis=0, tiled=True)  35.7 us
    all_to_all x1, waiting for transfers between devices, pack_attention(): lax.all_to_all(outgoing, 'blk', split_axis=0, concat_axis=0, tiled=True)  17.5 us
    another operation x1, loops' own time, prompt_attention(): lax.fori_loop(0, piece_rows // step_rows, one_step, init)  10.4 us
    all_to_all x1, starting transfers between devices, pack_attention(): lax.all_to_all(outgoing, 'blk', split_axis=0, concat_axis=0, tiled=True)  8.45 us
  transfers between devices with their start and end apart: 5, of which 4 were waited for; matrix products, arithmetic and copies ran while one was open for 12% of the time, Pallas kernels for 0%

commit v1 on v0

--- a/solution.py
+++ b/solution.py
@@ -43,7 +43,9 @@
         jnp.full((heads_dev, row_count), very_negative, jnp.float32),
         jnp.zeros((heads_dev, row_count), jnp.float32),
     )
-    key_piece = lax.all_gather(long_k, "blk", axis=0, tiled=True)
+    key_piece = jnp.concatenate(
+        lax.all_to_all(jnp.stack([long_k] * lax.axis_size("blk")), "blk", 0, 0), axis=0
+    )
     value_piece = lax.all_gather(long_v, "blk", axis=0, tiled=True)
     piece_rows = key_piece.shape[0]
     step_rows = math.gcd(piece_rows, 1024)

time: 405 us -> 432 us (1.067)
  local copies, waits for them, and re-layouts: 14.8 us -> 40.1 us
  starting transfers between devices: 8.79 us -> 14.9 us
  waiting for transfers between devices: 316 us -> 311 us
    all_to_all x0 -> x1, waiting for transfers between devices: none -> 121 us  [prompt_attention(): lax.all_to_all(jnp.stack([long_k] * lax.axis_size('blk')), 'blk', 0, 0)]
    all_gather x1, waiting for transfers between devices: 73.6 us -> 0.01 us  [prompt_attention(): value_piece = lax.all_gather(long_v, 'blk', axis=0, tiled=True)]
    all_gather x1 -> x0, waiting for transfers between devices: 35.7 us -> none  [prompt_attention(): key_piece = lax.all_gather(long_k, 'blk', axis=0, tiled=True)]
    reduce_scatter x1, waiting for transfers between devices: 189 us -> 171 us  [per_device(): lax.psum_scatter(jnp.dot(long_attn, w_rows, preferred_element_type=jnp.fl...]
    all_to_all x0 -> x1, local copies, waits for them, and re-layouts: none -> 12.3 us  [prompt_attention(): lax.all_to_all(jnp.stack([long_k] * lax.axis_size('blk')), 'blk', 0, 0)]
    unnamed x19 -> x22, local copies, waits for them, and re-layouts: 5.82 us -> 17 us
    all_to_all x0 -> x1, starting transfers between devices: none -> 6.18 us  [prompt_attention(): lax.all_to_all(jnp.stack([long_k] * lax.axis_size('blk')), 'blk', 0, 0)]
  transfers between devices with their start and end apart: 5 -> 5, of which waited for: 4 -> 3; matrix products, arithmetic and copies ran while one was open for 12% -> 17% of each run, Pallas kernels for 0% -> 0%
where the time goes in v1:
time: 432 us; the launch traced here: 430 us
  waiting for transfers between devices  311 us (72%)
  local copies, waits for them, and re-layouts  40.1 us (9%)
  matrix products  27.9 us (6%)
  between operations  15.8 us (4%)
  starting transfers between devices  14.9 us (3%)
  loops' own time  11.7 us (3%)
  other arithmetic  8.48 us (2%)
    reduce_scatter x1, waiting for transfers between devices, per_device(): lax.psum_scatter(jnp.dot(long_attn, w_rows, preferred_element_type=jnp.fl...  171 us
    all_to_all x1, waiting for transfers between devices, prompt_attention(): lax.all_to_all(jnp.stack([long_k] * lax.axis_size('blk')), 'blk', 0, 0)  121 us
    all_to_all x1, waiting for transfers between devices, pack_attention(): lax.all_to_all(outgoing, 'blk', split_axis=0, concat_axis=0, tiled=True)  19.3 us
    unnamed x22, local copies, waits for them, and re-layouts  17 us
    all_to_all x1, local copies, waits for them, and re-layouts, prompt_attention(): lax.all_to_all(jnp.stack([long_k] * lax.axis_size('blk')), 'blk', 0, 0)  12.3 us
    another operation x1, loops' own time, prompt_attention(): lax.fori_loop(0, piece_rows // step_rows, one_step, init)  11.3 us
  transfers between devices with their start and end apart: 5, of which 3 were waited for; matrix products, arithmetic and copies ran while one was open for 17% of the time, Pallas kernels for 0%

profile of v1, /device:TPU:1, one launch (start us, length us, event | category | flops | bytes accessed | tf_op | source)
XLA Modules:
  0.0 430.3 jit_solution(6280213818727028009)
XLA Ops:
  8.1 2.1 copy.85
  10.2 0.8 copy.89
  11.1 0.2 reduce_window_sum.11
  11.4 0.1 select_reduce_fusion
  11.5 0.1 copy.94
  11.6 0.1 reshape.285
  11.7 1.7 gather_fusion
  13.4 8.4 %all-to-all-start.1 = ((bf16[16,4,2,16,256]{4,3,2,1,0:T(8,128)(2,1)}), bf16[16,4,2,16,256]{4,3,2,1,0:T(8,128)(2,1)S(1)}, u32[]{:S(2)}, u32[]{:S(2)}) async-start(bf16[16,4,2,16,256]{4,3,2,1,0:T(8,128)(2,1)} %bitcast.10), calls=%async_computation.2 | async-start | bytes 2097152 | tf_op jit(solution)/shard_map/all_to_all | solution.py:92
  21.8 1.2 copy.82
  23.1 19.3 %all-to-all-done.1 = bf16[16,4,2,16,256]{4,3,2,1,0:T(8,128)(2,1)S(1)} async-done(((bf16[16,4,2,16,256]{4,3,2,1,0:T(8,128)(2,1)}), bf16[16,4,2,16,256]{4,3,2,1,0:T(8,128)(2,1)S(1)}, u32[]{:S(2)}, u32[]{:S(2)}) %all-to-all-start.1) | async-done | bytes 1048608 | tf_op jit(solution)/shard_map/all_to_all | solution.py:92
  42.4 4.3 stack.2
  46.6 6.2 %all-to-all-start = ((bf16[16,1024,256]{1,2,0:T(8,128)(2,1)}), bf16[16,1024,256]{1,2,0:T(8,128)(2,1)}, u32[]{:S(2)}, u32[]{:S(2)}) async-start(bf16[16,1024,256]{1,2,0:T(8,128)(2,1)} %stack.2), calls=%async_computation | async-start | bytes 16777216 | tf_op jit(solution)/shard_map/all_to_all | solution.py:47
  52.9 0.1 copy.95
  53.0 0.2 copy.97
  53.2 0.1 copy.99
  53.4 0.2 convert_reduce_fusion
  53.6 1.2 fusion.20
  54.8 0.6 gather_fusion.1
  55.5 0.1 concatenate.21
  55.7 0.1 concatenate.24
  55.9 0.4 copy.100
  56.3 6.1 %fusion.65 = (f32[2,512]{1,0:T(2,128)S(1)}, bf16[2,512,1536]{1,2,0:T(8,128)(2,1)}) fusion(pred[512,1536]{0,1:T(8,128)(4,1)S(1)} %fusion.20, bf16[512,2,128]{2,0,1:T(8,128)(2,1)S(1)} %copy.97, bf16[1024,2,128]{2,0,1:T(8,128)(2,1)S(1)} %copy.96, bf16[512,256]{1,0:T(8,128)(2,1)} %param.17), kind=kOutput, calls=%fused_computation.93 | convolution fusion | flops 413664768 | bytes 4984832 | tf_op jit(solution)/shard_map/sub | solution.py:116
  62.4 2.5 fusion.28
  65.0 3.3 convolution_convert_fusion.1
  68.3 0.2 reduce-scatter.3.cloned.1.call-start
  68.6 0.7 add_reduce_fusion
  69.3 0.2 copy.84
  69.5 0.3 copy.87
  69.7 121.1 %all-to-all-done = bf16[16,1024,256]{1,2,0:T(8,128)(2,1)} async-done(((bf16[16,1024,256]{1,2,0:T(8,128)(2,1)}), bf16[16,1024,256]{1,2,0:T(8,128)(2,1)}, u32[]{:S(2)}, u32[]{:S(2)}) %all-to-all-start) | async-done | bytes 8388640 | tf_op jit(solution)/shard_map/all_to_all | solution.py:47
  190.8 12.3 %copy.83 = bf16[16,1024,256]{2,1,0:T(8,128)(2,1)} copy(bf16[16,1024,256]{1,2,0:T(8,128)(2,1)} %all-to-all-done) | data formatting | bytes 16777216 | tf_op jit(solution)/shard_map/all_to_all | solution.py:47
  203.1 12.0 %copy.86 = bf16[16384,256]{0,1:T(8,128)(2,1)} copy(bf16[16384,256]{1,0:T(8,128)(2,1)} %bitcast.76) | data formatting | bytes 16777216
  215.2 31.6 %while.18 = (s32[]{:T(128)}, f32[2,1024,128]{2,1,0:T(8,128)S(1)}, f32[2,1024]{1,0:T(2,128)S(1)}, f32[2,1024]{1,0:T(2,128)S(1)}, s32[]{:T(128)}, /*index=5*/bf16[...) while((s32[]{:T(128)}, f32[2,1024,128]{2,1,0:T(8,128)S(1)}, ...), condition=%wide.region_6.7_spmd.clone, body=%wide.region_1.6_spmd.clone.sunk | while | flops 1102583808 | bytes 35283264 | solution.py:68
  215.9 10.0 %conditional.3 = ((f32[2,1024,128]{2,1,0:T(8,128)S(1)}, f32[2,1024]{1,0:T(2,128)S(1)}, f32[2,1024]{1,0:T(2,128)S(1)})) conditional(s32[]{:T(128)} %convert_element_type.77, (f32[2,1024,128]{2,1,0:T(8,128)S(1)}, f32[2,1024]{1,0:T(2,128)S(1)}, f32[2,1024]{1,0:T(2,128)S(1)}) %tuple.68, (s32[]{:T(128)}, s32[]{:T(128)}, bf16[16384,256]{0,1:T(8,128)(2,1)}, ...), branch_computations={%region_2.0_spmd, %region_3.5_spmd} | conditional | flops 1102583808 | bytes 35278928 | solution.py:66
  215.9 1.3 constant_dynamic-slice_fusion
  217.2 0.7 broadcast_compare_fusion
  217.9 2.0 fusion.2
  219.9 2.3 fusion.3
  222.2 3.7 fusion.8
  226.6 10.0 %conditional.3 = ((f32[2,1024,128]{2,1,0:T(8,128)S(1)}, f32[2,1024]{1,0:T(2,128)S(1)}, f32[2,1024]{1,0:T(2,128)S(1)})) conditional(s32[]{:T(128)} %convert_element_type.77, (f32[2,1024,128]{2,1,0:T(8,128)S(1)}, f32[2,1024]{1,0:T(2,128)S(1)}, f32[2,1024]{1,0:T(2,128)S(1)}) %tuple.68, (s32[]{:T(128)}, s32[]{:T(128)}, bf16[16384,256]{0,1:T(8,128)(2,1)}, ...), branch_computations={%region_2.0_spmd, %region_3.5_spmd} | conditional | flops 1102583808 | bytes 35278928 | solution.py:66
  226.6 1.3 constant_dynamic-slice_fusion
  227.9 0.7 broadcast_compare_fusion
  228.6 2.0 fusion.2
  230.6 2.3 fusion.3
  232.9 3.7 fusion.8
  246.8 0.3 copy.88
  247.1 0.1 divide_convert_fusion
  247.2 4.5 %convolution_convert_fusion = bf16[1024,2048]{1,0:T(8,128)(2,1)} fusion(bf16[1024,256]{0,1:T(8,128)(2,1)S(1)} %bitcast.80, bf16[2048,2048]{1,0:T(8,128)(2,1)} %param.23, s32[]{:T(128)S(6)} %select_n.90), kind=kOutput, calls=%fused_computation.25 | convolution fusion | flops 1075838976 | bytes 5767172 | tf_op jit(solution)/shard_map/dot_general | solution.py:142
  251.8 171.1 %reduce-scatter.3.cloned.1.call-done = bf16[128,2048]{1,0:T(8,128)(2,1)} async-done(((bf16[1024,2048]{1,0:T(8,128)(2,1)}), bf16[128,2048]{1,0:T(8,128)(2,1)}) %reduce-scatter.3.cloned.1.call-update) | async-done | bytes 524304 | tf_op jit(solution)/shard_map/reduce_scatter | solution.py:141
  (75 shorter events, 0.9 us)
Async XLA Ops:
  8.0 3.7 copy-start
  8.0 207.1 %all-gather.2.cloned.1.call-start = ((), (), s32[]{:S(2)}) async-start(), calls=%async_computation.4 | async-start | bytes 8912896 | tf_op jit(solution)/shard_map/all_gather | solution.py:49
  13.4 29.0 %all-to-all-start.1 = ((bf16[16,4,2,16,256]{4,3,2,1,0:T(8,128)(2,1)}), bf16[16,4,2,16,256]{4,3,2,1,0:T(8,128)(2,1)S(1)}, u32[]{:S(2)}, u32[]{:S(2)}) async-start(bf16[16,4,2,16,256]{4,3,2,1,0:T(8,128)(2,1)} %bitcast.10), calls=%async_computation.2 | async-start | bytes 2097152 | tf_op jit(solution)/shard_map/all_to_all | solution.py:92
  46.6 6.2 %copy-start.3 = (bf16[512,256]{1,0:T(8,128)(2,1)S(1)}, bf16[512,256]{1,0:T(8,128)(2,1)}, u32[]{:S(2)}) copy-start(bf16[512,256]{1,0:T(8,128)(2,1)} %param.18) | copy-start | bytes 786436
  46.6 6.6 %copy-start.4 = (bf16[512,256]{1,0:T(8,128)(2,1)S(1)}, bf16[512,256]{1,0:T(8,128)(2,1)}, u32[]{:S(2)}) copy-start(bf16[512,256]{1,0:T(8,128)(2,1)} %param.19) | copy-start | bytes 786436
  46.6 7.0 %copy-start.6 = (s32[1,512]{1,0:T(1,128)S(1)}, s32[1,512]{1,0:T(1,128)}, u32[]{:S(2)}) copy-start(s32[1,512]{1,0:T(1,128)} %param.20) | copy-start | bytes 6148
  46.6 7.0 %copy-start.5 = (s32[1536]{0:T(1024)S(1)}, s32[1536]{0:T(1024)}, u32[]{:S(2)}) copy-start(s32[1536]{0:T(1024)} %constant.138.clone.1) | copy-start | bytes 18436
  46.6 144.2 %all-to-all-start = ((bf16[16,1024,256]{1,2,0:T(8,128)(2,1)}), bf16[16,1024,256]{1,2,0:T(8,128)(2,1)}, u32[]{:S(2)}, u32[]{:S(2)}) async-start(bf16[16,1024,256]{1,2,0:T(8,128)(2,1)} %stack.2), calls=%async_computation | async-start | bytes 16777216 | tf_op jit(solution)/shard_map/all_to_all | solution.py:47
  52.8 198.9 %reduce-scatter.5.cloned.1.call-start = ((), (), s32[]{:S(2)}) async-start(), calls=%async_computation.6 | async-start | bytes 2359296 | tf_op jit(solution)/shard_map/reduce_scatter | solution.py:147
  62.4 6.8 %copy-start.2 = (bf16[1024,256]{1,0:T(8,128)(2,1)S(1)}, bf16[1024,256]{1,0:T(8,128)(2,1)}, u32[]{:S(2)}) copy-start(bf16[1024,256]{1,0:T(8,128)(2,1)} %param.14) | copy-start | bytes 1572868
  68.3 354.5 %reduce-scatter.3.cloned.1.call-start = ((), (), s32[]{:S(2)}) async-start(), calls=%async_computation.5 | async-start | bytes 4718592 | tf_op jit(solution)/shard_map/reduce_scatter | solution.py:141
  246.8 176.1 %copy-start.1 = (bf16[64,2,16,256]{3,2,1,0:T(8,128)(2,1)S(1)}, bf16[64,2,16,256]{3,2,1,0:T(8,128)(2,1)}, u32[]{:S(2)}) copy-start(bf16[64,2,16,256]{3,2,1,0:T(8,128)(2,1)} %param.21) | copy-start | bytes 3145732
Sparse Core Ops, SparseCore 0:
  11.9 177.9 all-gather.1
Sparse Core Ops, SparseCore 1:
  68.4 119.3 reduce-scatter.4
  251.8 170.9 reduce-scatter.2
